TPU v7x, 512 devices: a whole 4x8x8 slice. The times are simulated.
512 devices in a mesh: seq: 128 (over z, y_hi, x, core), head: 4 (over y_lo).
Axes of the slice: x: 4, y: 8 (y_hi: 2, y_lo: 4; y = y_hi * 4 + y_lo), z: 8, core: 2. Of those that a mesh axis runs over, the one named last changes fastest.
Arguments:
- query_rows: bfloat16 [32768, 8, 128], P('seq', 'head'), may hold values from -20 to 20
- key_rows: bfloat16 [32768, 8, 128], P('seq', 'head'), may hold values from -20 to 20
- value_rows: bfloat16 [32768, 8, 128], P('seq', 'head'), may hold values from -6 to 6
- cotangent: bfloat16 [32768, 8, 128], P('seq', 'head'), may hold values from -6 to 6
- norm_gain: float32 [8, 128], P('head'), may hold values from 0.5 to 2
- offsets: int32 [8], P('head'), may hold values from 0 to 31, as said below
Outputs:
- query_grad: bfloat16 [32768, 8, 128], P('seq', 'head')
- key_grad: bfloat16 [32768, 8, 128], P('seq', 'head')
- value_grad: bfloat16 [32768, 8, 128], P('seq', 'head')
Inputs may be any that keep to these rules, and one draw needn't show every extreme that they name: The heads' offsets are distinct.
All inputs are finite; a program needn't handle non-finite values.
Results may differ from a plain program's by a relative error of at most 0.018.
Values may be sent and summed in bfloat16 or wider, within the bound.
No kernel may reach another device: no remote copies, remote signals or barrier semaphores. Data moves between devices by JAX's collectives and lax.ppermute only.
A program may use at most 128 MiB of HBM per device.

v0:
```python
import jax
import jax.numpy as jnp
from jax import lax
from jax.sharding import PartitionSpec as P

RATE2 = 4
RATE3 = 16
RATE4 = 32


neg_fill = -1e30
epsilon = 1e-05
block_width = 512


def passed_along(value, axis, steps):
    count = lax.axis_size(axis)
    leading, last = (max(0, -steps), min(count, count - steps))
    return lax.ppermute(value, axis, [(source, source + steps) for source in range(leading, last)])


def pick_rows(source, wanted, stride):
    row_count = source.shape[0] // stride
    shaped = source.reshape((row_count, stride) + source.shape[1:])
    trailing = (1,) * (source.ndim - 2)
    target = wanted.reshape((1, 1, -1) + trailing)
    column = jnp.arange(stride, dtype=jnp.int32).reshape((1, stride, 1) + trailing)
    zeroed = jnp.where(column == target, shaped, jnp.zeros((), source.dtype))
    return jnp.sum(zeroed, axis=1, dtype=source.dtype)


def put_rows(compact, wanted, stride, filler):
    trailing = (1,) * (compact.ndim - 2)
    target = wanted.reshape((1, 1, -1) + trailing)
    column = jnp.arange(stride, dtype=jnp.int32).reshape((1, stride, 1) + trailing)
    spread = jnp.where(column == target, compact[:, None], jnp.asarray(filler, compact.dtype))
    return spread.reshape((compact.shape[0] * stride,) + compact.shape[1:])


def row_places(device, slot_count, direction, row_count, stride, wanted, tok_dev):
    owners = device + direction * jnp.arange(slot_count, dtype=jnp.int32)
    within_dev = wanted[None, :] + stride * jnp.arange(row_count, dtype=jnp.int32)[:, None]
    places = owners[:, None, None] * tok_dev + within_dev[None]
    return places.reshape(slot_count * row_count, wanted.shape[0])


def masked_scores(query_blk, key_blk, query_pos, key_pos, seg_len, score_scale):
    raw = (
        jnp.einsum("qhd,khd->hqk", query_blk, key_blk, preferred_element_type=jnp.float32)
        * score_scale
    )
    query_at = query_pos.T[:, :, None]
    key_at = key_pos.T[:, None, :]
    linked = (query_at // seg_len == key_at // seg_len) & (key_at <= query_at)
    return jnp.where(linked, raw, neg_fill)


def flatten_slots(member):
    return member.reshape((member.shape[0] * member.shape[1],) + member.shape[2:])


def extend(buffers, target, sign, puller):
    while buffers[0].shape[0] < target:
        covered = buffers[0].shape[0]
        arrived = puller(buffers, sign * covered)
        buffers = tuple(
            (jnp.concatenate([held, current], axis=0) for held, current in zip(buffers, arrived))
        )
    return buffers


def pull_keys(buffers, offset):
    return passed_along((buffers[0], buffers[1]), "seq", offset)


def pull_queries(buffers, offset):
    moved = passed_along((buffers[0], buffers[1]), "seq", offset)
    stats = passed_along((buffers[2], buffers[3]), "seq", offset)
    return (moved[0], moved[1], stats[0], stats[1])


def feature_sums(first, second):
    return lax.psum((first, second), "head")


def shards(query_rows, key_rows, value_rows, cotangent, norm_gain, offsets):
    tok_dev, heads_dev, head_size = query_rows.shape
    seq_count = lax.axis_size("seq")
    device = lax.axis_index("seq")
    group_rows = tok_dev * seq_count // RATE4
    score_scale = head_size ** (-0.5)
    features = heads_dev * head_size * lax.axis_size("head")
    levels = []
    for stride in (1, RATE2, RATE3, RATE4):
        seg_len = stride * group_rows
        levels.append((stride, seg_len, max(1, seg_len // tok_dev), offsets % stride))
    key_sets = []
    for stride, seg_len, span_devices, wanted in levels:
        own_rows = (
            pick_rows(key_rows, wanted, stride)[None],
            pick_rows(value_rows, wanted, stride)[None],
        )
        key_sets.append(extend(own_rows, span_devices, 1, pull_keys))
    prepared = []
    for (stride, seg_len, span_devices, wanted), key_set in zip(levels, key_sets):
        row_count = tok_dev // stride
        key_flat = flatten_slots(key_set[0])
        value_flat = flatten_slots(key_set[1])
        key_places = row_places(device, key_set[0].shape[0], -1, row_count, stride, wanted, tok_dev)
        query_sel = pick_rows(query_rows, wanted, stride)
        query_places = row_places(device, 1, -1, row_count, stride, wanted, tok_dev)
        prepared.append(
            (
                stride,
                seg_len,
                span_devices,
                wanted,
                row_count,
                key_flat,
                value_flat,
                key_places,
                query_sel,
                query_places,
            )
        )
    lse_total = jnp.full((tok_dev, heads_dev), neg_fill, jnp.float32)
    for (
        stride,
        seg_len,
        span_devices,
        wanted,
        row_count,
        key_flat,
        value_flat,
        key_places,
        query_sel,
        query_places,
    ) in prepared:
        level_lse = jnp.full((row_count, heads_dev), neg_fill, jnp.float32)
        for first_row in range(0, key_flat.shape[0], block_width):
            scores = masked_scores(
                query_sel,
                key_flat[first_row : first_row + block_width],
                query_places,
                key_places[first_row : first_row + block_width],
                seg_len,
                score_scale,
            )
            row_peak = jnp.max(scores, axis=2)
            block_lse = row_peak + jnp.log(jnp.sum(jnp.exp(scores - row_peak[:, :, None]), axis=2))
            level_lse = jnp.logaddexp(level_lse, block_lse.T)
        lse_total = jnp.logaddexp(lse_total, put_rows(level_lse, wanted, stride, neg_fill))
    attended = jnp.zeros((tok_dev, heads_dev, head_size), jnp.float32)
    for (
        stride,
        seg_len,
        span_devices,
        wanted,
        row_count,
        key_flat,
        value_flat,
        key_places,
        query_sel,
        query_places,
    ) in prepared:
        lse_sel = pick_rows(lse_total, wanted, stride)
        out_sel = jnp.zeros((row_count, heads_dev, head_size), jnp.float32)
        for first_row in range(0, key_flat.shape[0], block_width):
            scores = masked_scores(
                query_sel,
                key_flat[first_row : first_row + block_width],
                query_places,
                key_places[first_row : first_row + block_width],
                seg_len,
                score_scale,
            )
            weights = jnp.exp(scores - lse_sel.T[:, :, None]).astype(jnp.bfloat16)
            out_sel = out_sel + jnp.einsum(
                "hqk,khd->qhd",
                weights,
                value_flat[first_row : first_row + block_width],
                preferred_element_type=jnp.float32,
            )
        attended = attended + put_rows(out_sel, wanted, stride, 0.0)
    totals = feature_sums(jnp.sum(attended, axis=(1, 2)), jnp.sum(attended * attended, axis=(1, 2)))
    centre = totals[0] / features
    variance = totals[1] / features - centre * centre
    inverse = lax.rsqrt(variance + epsilon)
    normed = (attended - centre[:, None, None]) * inverse[:, None, None]
    grad_in = cotangent.astype(jnp.float32) * norm_gain[None]
    moments = feature_sums(jnp.sum(grad_in, axis=(1, 2)), jnp.sum(grad_in * normed, axis=(1, 2)))
    first_mean = moments[0] / features
    second_mean = moments[1] / features
    d_attended = (
        inverse[:, None, None]
        * (grad_in - first_mean[:, None, None] - normed * second_mean[:, None, None])
    ).astype(jnp.bfloat16)
    row_delta = jnp.sum(d_attended.astype(jnp.float32) * attended, axis=2)
    query_grad = jnp.zeros((tok_dev, heads_dev, head_size), jnp.float32)
    for (
        stride,
        seg_len,
        span_devices,
        wanted,
        row_count,
        key_flat,
        value_flat,
        key_places,
        query_sel,
        query_places,
    ) in prepared:
        lse_sel = pick_rows(lse_total, wanted, stride)
        dout_sel = pick_rows(d_attended, wanted, stride)
        delta_sel = pick_rows(row_delta, wanted, stride)
        grad_sel = jnp.zeros((row_count, heads_dev, head_size), jnp.float32)
        for first_row in range(0, key_flat.shape[0], block_width):
            key_block = key_flat[first_row : first_row + block_width]
            scores = masked_scores(
                query_sel,
                key_block,
                query_places,
                key_places[first_row : first_row + block_width],
                seg_len,
                score_scale,
            )
            weights = jnp.exp(scores - lse_sel.T[:, :, None])
            weight_grad = jnp.einsum(
                "qhd,khd->hqk",
                dout_sel,
                value_flat[first_row : first_row + block_width],
                preferred_element_type=jnp.float32,
            )
            score_grad = (weights * (weight_grad - delta_sel.T[:, :, None])).astype(jnp.bfloat16)
            grad_sel = grad_sel + jnp.einsum(
                "hqk,khd->qhd", score_grad, key_block, preferred_element_type=jnp.float32
            )
        query_grad = query_grad + put_rows(grad_sel * score_scale, wanted, stride, 0.0)
    query_sets = []
    for stride, seg_len, span_devices, wanted in levels:
        own_rows = (
            pick_rows(query_rows, wanted, stride)[None],
            pick_rows(d_attended, wanted, stride)[None],
            pick_rows(lse_total, wanted, stride)[None],
            pick_rows(row_delta, wanted, stride)[None],
        )
        query_sets.append(extend(own_rows, span_devices, -1, pull_queries))
    key_grad = jnp.zeros((tok_dev, heads_dev, head_size), jnp.float32)
    value_grad = jnp.zeros((tok_dev, heads_dev, head_size), jnp.float32)
    for (
        stride,
        seg_len,
        span_devices,
        wanted,
        row_count,
        key_flat,
        value_flat,
        key_places,
        query_sel,
        query_places,
    ), query_set in zip(prepared, query_sets):
        query_flat = flatten_slots(query_set[0])
        dout_flat = flatten_slots(query_set[1])
        lse_flat = flatten_slots(query_set[2])
        delta_flat = flatten_slots(query_set[3])
        query_far = row_places(device, query_set[0].shape[0], 1, row_count, stride, wanted, tok_dev)
        key_sel = pick_rows(key_rows, wanted, stride)
        value_sel = pick_rows(value_rows, wanted, stride)
        key_grad_sel = jnp.zeros((row_count, heads_dev, head_size), jnp.float32)
        value_grad_sel = jnp.zeros((row_count, heads_dev, head_size), jnp.float32)
        for first_row in range(0, query_flat.shape[0], block_width):
            query_block = query_flat[first_row : first_row + block_width]
            dout_block = dout_flat[first_row : first_row + block_width]
            lse_block = lse_flat[first_row : first_row + block_width]
            delta_block = delta_flat[first_row : first_row + block_width]
            scores = masked_scores(
                query_block,
                key_sel,
                query_far[first_row : first_row + block_width],
                query_places,
                seg_len,
                score_scale,
            )
            weights = jnp.exp(scores - lse_block.T[:, :, None])
            value_grad_sel = value_grad_sel + jnp.einsum(
                "hqk,qhd->khd",
                weights.astype(jnp.bfloat16),
                dout_block,
                preferred_element_type=jnp.float32,
            )
            weight_grad = jnp.einsum(
                "qhd,khd->hqk", dout_block, value_sel, preferred_element_type=jnp.float32
            )
            score_grad = (weights * (weight_grad - delta_block.T[:, :, None])).astype(jnp.bfloat16)
            key_grad_sel = key_grad_sel + jnp.einsum(
                "hqk,qhd->khd", score_grad, query_block, preferred_element_type=jnp.float32
            )
        key_grad = key_grad + put_rows(key_grad_sel * score_scale, wanted, stride, 0.0)
        value_grad = value_grad + put_rows(value_grad_sel, wanted, stride, 0.0)
    return (
        query_grad.astype(jnp.bfloat16),
        key_grad.astype(jnp.bfloat16),
        value_grad.astype(jnp.bfloat16),
    )


def solution(mesh):
    placed = (
        P("seq", "head", None),
        P("seq", "head", None),
        P("seq", "head", None),
        P("seq", "head", None),
        P("head", None),
        P("head"),
    )
    return jax.shard_map(
        shards,
        mesh=mesh,
        in_specs=placed,
        out_specs=(P("seq", "head", None), P("seq", "head", None), P("seq", "head", None)),
        check_vma=False,
    )
```

profile of v0, /device:TPU:104, one launch (start us, length us, event | category | flops | bytes accessed | tf_op | source)
XLA Modules:
  0.0 889.8 jit_solution(9926591408798527712)
XLA Ops:
  41.3 8.4 collective-permute-start.86
  55.4 9.7 %collective-permute-start.62 = (bf16[1,16,2,128]{3,1,2,0:T(8,128)(2,1)S(1)}, bf16[1,16,2,128]{3,1,2,0:T(8,128)(2,1)S(1)}, u32[]{:S(2)}, u32[]{:S(2)}) collective-permute-start(bf16[1,16,2,128]{3,1,2,0:T(8,128)(2,1)S(1)} %bitcast.580), channel_id=1, source_target_pairs={{4,0},{8,4},{12,8},{16,12},{20,16},{24,20},{28,24},{32,28},{36,32}... | collective-permute-start | bytes 24584 | tf_op jit(solution)/shard_map/ppermute | solution.py:19
  70.2 7.8 collective-permute-done.32
  80.5 9.0 %collective-permute-done.13 = bf16[2,8,2,128]{3,1,2,0:T(8,128)(2,1)S(1)} collective-permute-done((bf16[2,8,2,128]{3,1,2,0:T(8,128)(2,1)S(1)}, bf16[2,8,2,128]{3,1,2,0:T(8,128)(2,1)S(1)}, u32[]{:S(2)}, u32[]{:S(2)}) %collective-permute-start.13) | collective-permute-done | bytes 8224 | tf_op jit(solution)/shard_map/ppermute | solution.py:19
  97.6 9.1 %collective-permute-done.7 = bf16[2,16,2,128]{3,1,2,0:T(8,128)(2,1)S(1)} collective-permute-done((bf16[2,16,2,128]{3,1,2,0:T(8,128)(2,1)S(1)}, bf16[2,16,2,128]{3,1,2,0:T(8,128)(2,1)S(1)}, u32[]{:S(2)}, u32[]{:S(2)}) %collective-permute-start.7) | collective-permute-done | bytes 16416 | tf_op jit(solution)/shard_map/ppermute | solution.py:19
  108.6 9.7 %collective-permute-done.26 = bf16[2,16,2,128]{3,1,2,0:T(8,128)(2,1)S(1)} collective-permute-done((bf16[2,16,2,128]{3,1,2,0:T(8,128)(2,1)S(1)}, bf16[2,16,2,128]{3,1,2,0:T(8,128)(2,1)S(1)}, u32[]{:S(2)}, u32[]{:S(2)}) %collective-permute-start.26) | collective-permute-done | bytes 16416 | tf_op jit(solution)/shard_map/ppermute | solution.py:19
  128.8 7.1 collective-permute-done.33
  141.4 6.4 collective-permute-done.14
  157.5 8.2 collective-permute-start.46
  165.8 5.0 collective-permute-start.8
  170.9 10.2 %collective-permute-start.27 = (bf16[4,16,2,128]{3,1,2,0:T(8,128)(2,1)S(1)}, bf16[4,16,2,128]{3,1,2,0:T(8,128)(2,1)S(1)}, u32[]{:S(2)}, u32[]{:S(2)}) collective-permute-start(bf16[4,16,2,128]{3,1,2,0:T(8,128)(2,1)S(1)} %pad_maximum_fusion.22), channel_id=1, source_target_pairs={{0,16},{4,20},{8,24},{12,28},{16,32},{20,36},{24,40},{28,44},{32,4... | collective-permute-start | bytes 98312 | tf_op jit(solution)/shard_map/ppermute | solution.py:19
  183.1 8.4 collective-permute-start.34
  191.5 5.3 collective-permute-start.15
  216.4 5.4 collective-permute-start.47
  222.5 14.0 %collective-permute-start.9 = (bf16[8,16,2,128]{3,1,2,0:T(8,128)(2,1)S(1)}, bf16[8,16,2,128]{3,1,2,0:T(8,128)(2,1)S(1)}, u32[]{:S(2)}, u32[]{:S(2)}) collective-permute-start(bf16[8,16,2,128]{3,1,2,0:T(8,128)(2,1)S(1)} %pad_maximum_fusion.13), channel_id=1, source_target_pairs={{0,32},{4,36},{8,40},{12,44},{16,48},{20,52},{24,56},{28,60},{32,6... | collective-permute-start | bytes 196616 | tf_op jit(solution)/shard_map/ppermute | solution.py:19
  236.5 8.4 collective-permute-start.28
  247.5 9.3 %collective-permute-start.35 = (bf16[16,8,2,128]{3,1,2,0:T(8,128)(2,1)S(1)}, bf16[16,8,2,128]{3,1,2,0:T(8,128)(2,1)S(1)}, u32[]{:S(2)}, u32[]{:S(2)}) collective-permute-start(bf16[16,8,2,128]{3,1,2,0:T(8,128)(2,1)S(1)} %get-tuple-element.80), channel_id=1, source_target_pairs={{0,64},{4,68},{8,72},{12,76},{16,80},{20,84},{24,88},{28,92},{32,9... | collective-permute-start | bytes 196616 | tf_op jit(solution)/shard_map/ppermute | solution.py:19
  257.4 6.2 collective-permute-start.16
  270.5 6.8 collective-permute-start.23
  278.0 5.3 collective-permute-start.48
  330.3 9.9 %collective-permute-start.42 = (bf16[2,256,2,128]{3,2,1,0:T(2,128)(2,1)S(1)}, bf16[2,256,2,128]{3,2,1,0:T(2,128)(2,1)}, u32[]{:S(2)}, u32[]{:S(2)}) collective-permute-start(bf16[2,256,2,128]{3,2,1,0:T(2,128)(2,1)S(1)} %pad_maximum_fusion.4), channel_id=1, source_target_pairs={{8,0},{12,4},{16,8},{20,12},{24,16},{28,20},{32,24},{36,28},{40,32... | collective-permute-start | bytes 786440 | tf_op jit(solution)/shard_map/ppermute | solution.py:19
  342.8 12.9 %collective-permute-start.5 = (bf16[8,64,2,128]{3,1,2,0:T(8,128)(2,1)}, bf16[8,64,2,128]{3,1,2,0:T(8,128)(2,1)}, u32[]{:S(2)}, u32[]{:S(2)}) collective-permute-start(bf16[8,64,2,128]{3,1,2,0:T(8,128)(2,1)} %pad_maximum_fusion.1), channel_id=1, source_target_pairs={{0,32},{4,36},{8,40},{12,44},{16,48},{20,52},{24,56},{28,60},{32,6... | collective-permute-start | bytes 786440 | tf_op jit(solution)/shard_map/ppermute | solution.py:19
  359.8 7.8 collective-permute-start.58
  368.4 5.0 collective-permute-start.11
  384.9 6.1 collective-permute-start.18
  432.7 11.5 %all-reduce.1 = (f32[256]{0:T(256)}, f32[256]{0:T(256)}) all-reduce(f32[256]{0:T(256)S(1)} %copy-done.195, f32[256]{0:T(256)S(1)} %copy-done.196), channel_id=1, replica_groups=mesh['seq'=128,'head'=4] {'head'}, use_global_device_ids=true, to_apply=%region_29.30 | all-reduce | flops 512 | bytes 4096 | tf_op jit(solution)/shard_map/psum | solution.py:83
  447.9 9.8 %all-reduce = (f32[256]{0:T(256)S(1)}, f32[256]{0:T(256)S(1)}) all-reduce(f32[256]{0:T(256)S(1)} %copy-done.198, f32[256]{0:T(256)S(1)} %copy-done.197), channel_id=1, replica_groups=mesh['seq'=128,'head'=4] {'head'}, use_global_device_ids=true, to_apply=%region_35.36 | all-reduce | flops 512 | bytes 4096 | tf_op jit(solution)/shard_map/psum | solution.py:83
  476.0 8.2 collective-permute-start.104
  529.8 7.9 collective-permute-start.105
  539.0 10.2 %collective-permute-start.68 = (f32[2,16,2]{1,2,0:T(2,128)S(1)}, f32[2,16,2]{1,2,0:T(2,128)S(1)}, u32[]{:S(2)}, u32[]{:S(2)}) collective-permute-start(f32[2,16,2]{1,2,0:T(2,128)S(1)} %pad_maximum_fusion.56), channel_id=1, source_target_pairs={{8,0},{12,4},{16,8},{20,12},{24,16},{28,20},{32,24},{36,28},{40,32... | collective-permute-start | bytes 776 | tf_op jit(solution)/shard_map/ppermute | solution.py:19
  550.5 10.2 %collective-permute-start.78 = (f32[2,16,2]{1,2,0:T(2,128)S(1)}, f32[2,16,2]{1,2,0:T(2,128)S(1)}, u32[]{:S(2)}, u32[]{:S(2)}) collective-permute-start(f32[2,16,2]{1,2,0:T(2,128)S(1)} %pad_maximum_fusion.57), channel_id=1, source_target_pairs={{8,0},{12,4},{16,8},{20,12},{24,16},{28,20},{32,24},{36,28},{40,32... | collective-permute-start | bytes 776 | tf_op jit(solution)/shard_map/ppermute | solution.py:19
  568.9 8.4 collective-permute-start.106
  578.7 11.4 %collective-permute-start.55 = (f32[1,64,2]{1,2,0:T(2,128)S(1)}, f32[1,64,2]{1,2,0:T(2,128)S(1)}, u32[]{:S(2)}, u32[]{:S(2)}) collective-permute-start(f32[1,64,2]{1,2,0:T(2,128)S(1)} %bitcast.659), channel_id=1, source_target_pairs={{4,0},{8,4},{12,8},{16,12},{20,16},{24,20},{28,24},{32,28},{36,32}... | collective-permute-start | bytes 1544 | tf_op jit(solution)/shard_map/ppermute | solution.py:19
  592.8 11.2 %collective-permute-start.79 = (f32[4,16,2]{1,2,0:T(2,128)S(1)}, f32[4,16,2]{1,2,0:T(2,128)S(1)}, u32[]{:S(2)}, u32[]{:S(2)}) collective-permute-start(f32[4,16,2]{1,2,0:T(2,128)S(1)} %pad_maximum_fusion.51), channel_id=1, source_target_pairs={{16,0},{20,4},{24,8},{28,12},{32,16},{36,20},{40,24},{44,28},{48,3... | collective-permute-start | bytes 1544 | tf_op jit(solution)/shard_map/ppermute | solution.py:19
  608.1 6.3 collective-permute-done.95
  614.4 8.1 collective-permute-start.50
  622.5 7.4 collective-permute-start.56
  650.7 6.9 collective-permute-start.98
  669.1 6.7 collective-permute-start.57
  680.2 10.7 %collective-permute-done.71 = f32[16,16,2]{1,2,0:T(2,128)S(1)} collective-permute-done((f32[16,16,2]{1,2,0:T(2,128)S(1)}, f32[16,16,2]{1,2,0:T(2,128)S(1)}, u32[]{:S(2)}, u32[]{:S(2)}) %collective-permute-start.71) | collective-permute-done | bytes 2080 | tf_op jit(solution)/shard_map/ppermute | solution.py:19
  701.0 7.4 collective-permute-done.97
  716.0 9.8 %collective-permute-start.43 = (f32[2,256,2]{1,2,0:T(2,128)S(1)}, f32[2,256,2]{1,2,0:T(2,128)S(1)}, u32[]{:S(2)}, u32[]{:S(2)}) collective-permute-start(f32[2,256,2]{1,2,0:T(2,128)S(1)} %pad_maximum_fusion.46), channel_id=1, source_target_pairs={{8,0},{12,4},{16,8},{20,12},{24,16},{28,20},{32,24},{36,28},{40,32... | collective-permute-start | bytes 12296 | tf_op jit(solution)/shard_map/ppermute | solution.py:19
  727.2 7.9 collective-permute-start.59
  770.2 5.8 collective-permute-done.113
  781.5 8.5 collective-permute-start.100
  793.2 7.0 collective-permute-start.101
  800.8 8.4 collective-permute-start.53
  859.3 20.3 %collective-permute-done.112 = bf16[64,8,2,128]{3,1,2,0:T(8,128)(2,1)} collective-permute-done((bf16[64,8,2,128]{3,1,2,0:T(8,128)(2,1)}, bf16[64,8,2,128]{3,1,2,0:T(8,128)(2,1)}, u32[]{:S(2)}, u32[]{:S(2)}) %collective-permute-start.112) | collective-permute-done | bytes 262176 | tf_op jit(solution)/shard_map/ppermute | solution.py:19
  (1092 shorter events, 473.5 us)
Async XLA Ops:
  0.6 277.4 %collective-permute-start = (bf16[1,256,2,128]{3,2,1,0:T(2,128)(2,1)}, bf16[1,256,2,128]{3,2,1,0:T(2,128)(2,1)S(1)}, u32[]{:S(2)}, u32[]{:S(2)}) collective-permute-start(bf16[1,256,2,128]{3,2,1,0:T(2,128)(2,1)} %bitcast.521), channel_id=1, source_target_pairs={{0,4},{4,8},{8,12},{12,16},{16,20},{20,24},{24,28},{28,32},{32,36}... | collective-permute-start | bytes 393224 | tf_op jit(solution)/shard_map/ppermute | solution.py:19
  4.0 33.5 %collective-permute-start.31 = (bf16[1,8,2,128]{3,1,2,0:T(8,128)(2,1)S(1)}, bf16[1,8,2,128]{3,1,2,0:T(8,128)(2,1)S(1)}, u32[]{:S(2)}, u32[]{:S(2)}) collective-permute-start(bf16[1,8,2,128]{3,1,2,0:T(8,128)(2,1)S(1)} %bitcast.593), channel_id=1, source_target_pairs={{0,4},{4,8},{8,12},{12,16},{16,20},{20,24},{24,28},{28,32},{32,36}... | collective-permute-start | bytes 12296 | tf_op jit(solution)/shard_map/ppermute | solution.py:19
  7.5 33.8 %collective-permute-start.12 = (bf16[1,8,2,128]{3,1,2,0:T(8,128)(2,1)S(1)}, bf16[1,8,2,128]{3,1,2,0:T(8,128)(2,1)S(1)}, u32[]{:S(2)}, u32[]{:S(2)}) collective-permute-start(bf16[1,8,2,128]{3,1,2,0:T(8,128)(2,1)S(1)} %bitcast.597), channel_id=1, source_target_pairs={{0,4},{4,8},{8,12},{12,16},{16,20},{20,24},{24,28},{28,32},{32,36}... | collective-permute-start | bytes 12296 | tf_op jit(solution)/shard_map/ppermute | solution.py:19
  9.8 43.6 %collective-permute-start.6 = (bf16[1,16,2,128]{3,1,2,0:T(8,128)(2,1)S(1)}, bf16[1,16,2,128]{3,1,2,0:T(8,128)(2,1)S(1)}, u32[]{:S(2)}, u32[]{:S(2)}) collective-permute-start(bf16[1,16,2,128]{3,1,2,0:T(8,128)(2,1)S(1)} %bitcast.584), channel_id=1, source_target_pairs={{0,4},{4,8},{8,12},{12,16},{16,20},{20,24},{24,28},{28,32},{32,36}... | collective-permute-start | bytes 24584 | tf_op jit(solution)/shard_map/ppermute | solution.py:19
  14.1 143.4 %collective-permute-start.2 = (bf16[1,64,2,128]{3,1,2,0:T(8,128)(2,1)S(1)}, bf16[1,64,2,128]{3,1,2,0:T(8,128)(2,1)S(1)}, u32[]{:S(2)}, u32[]{:S(2)}) collective-permute-start(bf16[1,64,2,128]{3,1,2,0:T(8,128)(2,1)S(1)} %bitcast.564), channel_id=1, source_target_pairs={{0,4},{4,8},{8,12},{12,16},{16,20},{20,24},{24,28},{28,32},{32,36}... | collective-permute-start | bytes 98312 | tf_op jit(solution)/shard_map/ppermute | solution.py:19
  37.5 17.9 %collective-permute-start.25 = (bf16[1,16,2,128]{3,1,2,0:T(8,128)(2,1)S(1)}, bf16[1,16,2,128]{3,1,2,0:T(8,128)(2,1)S(1)}, u32[]{:S(2)}, u32[]{:S(2)}) collective-permute-start(bf16[1,16,2,128]{3,1,2,0:T(8,128)(2,1)S(1)} %bitcast.576), channel_id=1, source_target_pairs={{0,4},{4,8},{8,12},{12,16},{16,20},{20,24},{24,28},{28,32},{32,36}... | collective-permute-start | bytes 24584 | tf_op jit(solution)/shard_map/ppermute | solution.py:19
  51.0 114.8 %collective-permute-start.21 = (bf16[1,64,2,128]{3,1,2,0:T(8,128)(2,1)S(1)}, bf16[1,64,2,128]{3,1,2,0:T(8,128)(2,1)S(1)}, u32[]{:S(2)}, u32[]{:S(2)}) collective-permute-start(bf16[1,64,2,128]{3,1,2,0:T(8,128)(2,1)S(1)} %bitcast.524), channel_id=1, source_target_pairs={{0,4},{4,8},{8,12},{12,16},{16,20},{20,24},{24,28},{28,32},{32,36}... | collective-permute-start | bytes 98312 | tf_op jit(solution)/shard_map/ppermute | solution.py:19
  53.5 230.3 %collective-permute-start.19 = (bf16[1,256,2,128]{3,2,1,0:T(2,128)(2,1)S(1)}, bf16[1,256,2,128]{3,2,1,0:T(2,128)(2,1)S(1)}, u32[]{:S(2)}, u32[]{:S(2)}) collective-permute-start(bf16[1,256,2,128]{3,2,1,0:T(2,128)(2,1)S(1)} %bitcast.487), channel_id=1, source_target_pairs={{0,4},{4,8},{8,12},{12,16},{16,20},{20,24},{24,28},{28,32},{32,36}... | collective-permute-start | bytes 393224 | tf_op jit(solution)/shard_map/ppermute | solution.py:19
  155.0 134.0 %collective-permute-start.38 = (bf16[1,256,2,128]{3,2,1,0:T(2,128)(2,1)S(1)}, bf16[1,256,2,128]{3,2,1,0:T(2,128)(2,1)S(1)}, u32[]{:S(2)}, u32[]{:S(2)}) collective-permute-start(bf16[1,256,2,128]{3,2,1,0:T(2,128)(2,1)S(1)} %bitcast.519), channel_id=1, source_target_pairs={{4,0},{8,4},{12,8},{16,12},{20,16},{24,20},{28,24},{32,28},{36,32}... | collective-permute-start | bytes 393224 | tf_op jit(solution)/shard_map/ppermute | solution.py:19
  216.4 20.1 %collective-permute-start.47 = (bf16[2,64,2,128]{3,1,2,0:T(8,128)(2,1)S(1)}, bf16[2,64,2,128]{3,1,2,0:T(8,128)(2,1)S(1)}, u32[]{:S(2)}, u32[]{:S(2)}) collective-permute-start(bf16[2,64,2,128]{3,1,2,0:T(8,128)(2,1)S(1)} %pad_maximum_fusion.16), channel_id=1, source_target_pairs={{8,0},{12,4},{16,8},{20,12},{24,16},{28,20},{32,24},{36,28},{40,32... | collective-permute-start | bytes 196616 | tf_op jit(solution)/shard_map/ppermute | solution.py:19
  222.5 22.4 %collective-permute-start.9 = (bf16[8,16,2,128]{3,1,2,0:T(8,128)(2,1)S(1)}, bf16[8,16,2,128]{3,1,2,0:T(8,128)(2,1)S(1)}, u32[]{:S(2)}, u32[]{:S(2)}) collective-permute-start(bf16[8,16,2,128]{3,1,2,0:T(8,128)(2,1)S(1)} %pad_maximum_fusion.13), channel_id=1, source_target_pairs={{0,32},{4,36},{8,40},{12,44},{16,48},{20,52},{24,56},{28,60},{32,6... | collective-permute-start | bytes 196616 | tf_op jit(solution)/shard_map/ppermute | solution.py:19
  247.5 16.8 %collective-permute-start.35 = (bf16[16,8,2,128]{3,1,2,0:T(8,128)(2,1)S(1)}, bf16[16,8,2,128]{3,1,2,0:T(8,128)(2,1)S(1)}, u32[]{:S(2)}, u32[]{:S(2)}) collective-permute-start(bf16[16,8,2,128]{3,1,2,0:T(8,128)(2,1)S(1)} %get-tuple-element.80), channel_id=1, source_target_pairs={{0,64},{4,68},{8,72},{12,76},{16,80},{20,84},{24,88},{28,92},{32,9... | collective-permute-start | bytes 196616 | tf_op jit(solution)/shard_map/ppermute | solution.py:19
  266.8 28.5 %collective-permute-start.4 = (bf16[4,64,2,128]{3,1,2,0:T(8,128)(2,1)}, bf16[4,64,2,128]{3,1,2,0:T(8,128)(2,1)}, u32[]{:S(2)}, u32[]{:S(2)}) collective-permute-start(bf16[4,64,2,128]{3,1,2,0:T(8,128)(2,1)} %pad_maximum_fusion.8), channel_id=1, source_target_pairs={{0,16},{4,20},{8,24},{12,28},{16,32},{20,36},{24,40},{28,44},{32,4... | collective-permute-start | bytes 393224 | tf_op jit(solution)/shard_map/ppermute | solution.py:19
  270.5 31.3 %collective-permute-start.23 = (bf16[4,64,2,128]{3,1,2,0:T(8,128)(2,1)S(1)}, bf16[4,64,2,128]{3,1,2,0:T(8,128)(2,1)}, u32[]{:S(2)}, u32[]{:S(2)}) collective-permute-start(bf16[4,64,2,128]{3,1,2,0:T(8,128)(2,1)S(1)} %pad_maximum_fusion.9), channel_id=1, source_target_pairs={{0,16},{4,20},{8,24},{12,28},{16,32},{20,36},{24,40},{28,44},{32,4... | collective-permute-start | bytes 393224 | tf_op jit(solution)/shard_map/ppermute | solution.py:19
  278.0 29.7 %collective-permute-start.48 = (bf16[4,64,2,128]{3,1,2,0:T(8,128)(2,1)S(1)}, bf16[4,64,2,128]{3,1,2,0:T(8,128)(2,1)}, u32[]{:S(2)}, u32[]{:S(2)}) collective-permute-start(bf16[4,64,2,128]{3,1,2,0:T(8,128)(2,1)S(1)} %pad_maximum_fusion.10), channel_id=1, source_target_pairs={{16,0},{20,4},{24,8},{28,12},{32,16},{36,20},{40,24},{44,28},{48,3... | collective-permute-start | bytes 393224 | tf_op jit(solution)/shard_map/ppermute | solution.py:19
  283.8 31.7 %collective-permute-start.10 = (bf16[16,16,2,128]{3,1,2,0:T(8,128)(2,1)}, bf16[16,16,2,128]{3,1,2,0:T(8,128)(2,1)}, u32[]{:S(2)}, u32[]{:S(2)}) collective-permute-start(bf16[16,16,2,128]{3,1,2,0:T(8,128)(2,1)} %get-tuple-element.62), channel_id=1, source_target_pairs={{0,64},{4,68},{8,72},{12,76},{16,80},{20,84},{24,88},{28,92},{32,9... | collective-permute-start | bytes 393224 | tf_op jit(solution)/shard_map/ppermute | solution.py:19
  289.0 31.5 %collective-permute-start.29 = (bf16[16,16,2,128]{3,1,2,0:T(8,128)(2,1)}, bf16[16,16,2,128]{3,1,2,0:T(8,128)(2,1)S(1)}, u32[]{:S(2)}, u32[]{:S(2)}) collective-permute-start(bf16[16,16,2,128]{3,1,2,0:T(8,128)(2,1)} %get-tuple-element.56), channel_id=1, source_target_pairs={{0,64},{4,68},{8,72},{12,76},{16,80},{20,84},{24,88},{28,92},{32,9... | collective-permute-start | bytes 393224 | tf_op jit(solution)/shard_map/ppermute | solution.py:19
  295.4 29.1 %collective-permute-start.66 = (bf16[16,16,2,128]{3,1,2,0:T(8,128)(2,1)S(1)}, bf16[16,16,2,128]{3,1,2,0:T(8,128)(2,1)S(1)}, u32[]{:S(2)}, u32[]{:S(2)}) collective-permute-start(bf16[16,16,2,128]{3,1,2,0:T(8,128)(2,1)S(1)} %copy-done.241), channel_id=1, source_target_pairs={{64,0},{68,4},{72,8},{76,12},{80,16},{84,20},{88,24},{92,28},{96,3... | collective-permute-start | bytes 393224 | tf_op jit(solution)/shard_map/ppermute | solution.py:19
  302.4 40.4 %collective-permute-start.36 = (bf16[32,8,2,128]{3,1,2,0:T(8,128)(2,1)S(1)}, bf16[32,8,2,128]{3,1,2,0:T(8,128)(2,1)S(1)}, u32[]{:S(2)}, u32[]{:S(2)}) collective-permute-start(bf16[32,8,2,128]{3,1,2,0:T(8,128)(2,1)S(1)} %copy-done.249), channel_id=1, source_target_pairs={{0,128},{4,132},{8,136},{12,140},{16,144},{20,148},{24,152},{28,15... | collective-permute-start | bytes 393224 | tf_op jit(solution)/shard_map/ppermute | solution.py:19
  307.8 22.6 %collective-permute-start.17 = (bf16[32,8,2,128]{3,1,2,0:T(8,128)(2,1)S(1)}, bf16[32,8,2,128]{3,1,2,0:T(8,128)(2,1)S(1)}, u32[]{:S(2)}, u32[]{:S(2)}) collective-permute-start(bf16[32,8,2,128]{3,1,2,0:T(8,128)(2,1)S(1)} %copy-done.247), channel_id=1, source_target_pairs={{0,128},{4,132},{8,136},{12,140},{16,144},{20,148},{24,152},{28,15... | collective-permute-start | bytes 393224 | tf_op jit(solution)/shard_map/ppermute | solution.py:19
  315.6 40.8 %collective-permute-start.91 = (bf16[32,8,2,128]{3,1,2,0:T(8,128)(2,1)S(1)}, bf16[32,8,2,128]{3,1,2,0:T(8,128)(2,1)S(1)}, u32[]{:S(2)}, u32[]{:S(2)}) collective-permute-start(bf16[32,8,2,128]{3,1,2,0:T(8,128)(2,1)S(1)} %copy-done.245), channel_id=1, source_target_pairs={{128,0},{132,4},{136,8},{140,12},{144,16},{148,20},{152,24},{156,2... | collective-permute-start | bytes 393224 | tf_op jit(solution)/shard_map/ppermute | solution.py:19
  320.5 39.3 %collective-permute-start.1 = (bf16[2,256,2,128]{3,2,1,0:T(2,128)(2,1)S(1)}, bf16[2,256,2,128]{3,2,1,0:T(2,128)(2,1)S(1)}, u32[]{:S(2)}, u32[]{:S(2)}) collective-permute-start(bf16[2,256,2,128]{3,2,1,0:T(2,128)(2,1)S(1)} %pad_maximum_fusion), channel_id=1, source_target_pairs={{0,8},{4,12},{8,16},{12,20},{16,24},{20,28},{24,32},{28,36},{32,40... | collective-permute-start | bytes 786440 | tf_op jit(solution)/shard_map/ppermute | solution.py:19
  324.6 43.8 %collective-permute-start.20 = (bf16[2,256,2,128]{3,2,1,0:T(2,128)(2,1)S(1)}, bf16[2,256,2,128]{3,2,1,0:T(2,128)(2,1)S(1)}, u32[]{:S(2)}, u32[]{:S(2)}) collective-permute-start(bf16[2,256,2,128]{3,2,1,0:T(2,128)(2,1)S(1)} %pad_maximum_fusion.2), channel_id=1, source_target_pairs={{0,8},{4,12},{8,16},{12,20},{16,24},{20,28},{24,32},{28,36},{32,40... | collective-permute-start | bytes 786440 | tf_op jit(solution)/shard_map/ppermute | solution.py:19
  330.3 44.9 %collective-permute-start.42 = (bf16[2,256,2,128]{3,2,1,0:T(2,128)(2,1)S(1)}, bf16[2,256,2,128]{3,2,1,0:T(2,128)(2,1)}, u32[]{:S(2)}, u32[]{:S(2)}) collective-permute-start(bf16[2,256,2,128]{3,2,1,0:T(2,128)(2,1)S(1)} %pad_maximum_fusion.4), channel_id=1, source_target_pairs={{8,0},{12,4},{16,8},{20,12},{24,16},{28,20},{32,24},{36,28},{40,32... | collective-permute-start | bytes 786440 | tf_op jit(solution)/shard_map/ppermute | solution.py:19
  342.8 36.9 %collective-permute-start.5 = (bf16[8,64,2,128]{3,1,2,0:T(8,128)(2,1)}, bf16[8,64,2,128]{3,1,2,0:T(8,128)(2,1)}, u32[]{:S(2)}, u32[]{:S(2)}) collective-permute-start(bf16[8,64,2,128]{3,1,2,0:T(8,128)(2,1)} %pad_maximum_fusion.1), channel_id=1, source_target_pairs={{0,32},{4,36},{8,40},{12,44},{16,48},{20,52},{24,56},{28,60},{32,6... | collective-permute-start | bytes 786440 | tf_op jit(solution)/shard_map/ppermute | solution.py:19
  356.4 28.4 %collective-permute-start.24 = (bf16[8,64,2,128]{3,1,2,0:T(8,128)(2,1)}, bf16[8,64,2,128]{3,1,2,0:T(8,128)(2,1)}, u32[]{:S(2)}, u32[]{:S(2)}) collective-permute-start(bf16[8,64,2,128]{3,1,2,0:T(8,128)(2,1)} %pad_maximum_fusion.3), channel_id=1, source_target_pairs={{0,32},{4,36},{8,40},{12,44},{16,48},{20,52},{24,56},{28,60},{32,6... | collective-permute-start | bytes 786440 | tf_op jit(solution)/shard_map/ppermute | solution.py:19
  359.8 32.1 %collective-permute-start.58 = (bf16[8,64,2,128]{3,1,2,0:T(8,128)(2,1)}, bf16[8,64,2,128]{3,1,2,0:T(8,128)(2,1)}, u32[]{:S(2)}, u32[]{:S(2)}) collective-permute-start(bf16[8,64,2,128]{3,1,2,0:T(8,128)(2,1)} %pad_maximum_fusion.6), channel_id=1, source_target_pairs={{32,0},{36,4},{40,8},{44,12},{48,16},{52,20},{56,24},{60,28},{64,3... | collective-permute-start | bytes 786440 | tf_op jit(solution)/shard_map/ppermute | solution.py:19
  368.4 27.2 %collective-permute-start.11 = (bf16[32,16,2,128]{3,1,2,0:T(8,128)(2,1)}, bf16[32,16,2,128]{3,1,2,0:T(8,128)(2,1)}, u32[]{:S(2)}, u32[]{:S(2)}) collective-permute-start(bf16[32,16,2,128]{3,1,2,0:T(8,128)(2,1)} %constant_dynamic-update-slice_fusion.5), channel_id=1, source_target_pairs={{0,128},{4,132},{8,136},{12,140},{16,144},{20,148},{24,152},{28,15... | collective-permute-start | bytes 786440 | tf_op jit(solution)/shard_map/ppermute | solution.py:19
  375.3 25.7 %collective-permute-start.30 = (bf16[32,16,2,128]{3,1,2,0:T(8,128)(2,1)S(1)}, bf16[32,16,2,128]{3,1,2,0:T(8,128)(2,1)}, u32[]{:S(2)}, u32[]{:S(2)}) collective-permute-start(bf16[32,16,2,128]{3,1,2,0:T(8,128)(2,1)S(1)} %copy-done.56), channel_id=1, source_target_pairs={{0,128},{4,132},{8,136},{12,140},{16,144},{20,148},{24,152},{28,15... | collective-permute-start | bytes 786440 | tf_op jit(solution)/shard_map/ppermute | solution.py:19
  379.7 22.9 %collective-permute-start.82 = (bf16[32,16,2,128]{3,1,2,0:T(8,128)(2,1)}, bf16[32,16,2,128]{3,1,2,0:T(8,128)(2,1)}, u32[]{:S(2)}, u32[]{:S(2)}) collective-permute-start(bf16[32,16,2,128]{3,1,2,0:T(8,128)(2,1)} %constant_dynamic-update-slice_fusion.63), channel_id=1, source_target_pairs={{128,0},{132,4},{136,8},{140,12},{144,16},{148,20},{152,24},{156,2... | collective-permute-start | bytes 786440 | tf_op jit(solution)/shard_map/ppermute | solution.py:19
  384.9 18.7 %collective-permute-start.18 = (bf16[64,8,2,128]{3,1,2,0:T(8,128)(2,1)}, bf16[64,8,2,128]{3,1,2,0:T(8,128)(2,1)}, u32[]{:S(2)}, u32[]{:S(2)}) collective-permute-start(bf16[64,8,2,128]{3,1,2,0:T(8,128)(2,1)} %constant_dynamic-update-slice_fusion.22), channel_id=1, source_target_pairs={{0,256},{4,260},{8,264},{12,268},{16,272},{20,276},{24,280},{28,28... | collective-permute-start | bytes 786440 | tf_op jit(solution)/shard_map/ppermute | solution.py:19
  391.9 23.6 %collective-permute-start.37 = (bf16[64,8,2,128]{3,1,2,0:T(8,128)(2,1)}, bf16[64,8,2,128]{3,1,2,0:T(8,128)(2,1)}, u32[]{:S(2)}, u32[]{:S(2)}) collective-permute-start(bf16[64,8,2,128]{3,1,2,0:T(8,128)(2,1)} %constant_dynamic-update-slice_fusion.51), channel_id=1, source_target_pairs={{0,256},{4,260},{8,264},{12,268},{16,272},{20,276},{24,280},{28,28... | collective-permute-start | bytes 786440 | tf_op jit(solution)/shard_map/ppermute | solution.py:19
  395.6 370.3 %collective-permute-start.110 = (bf16[64,8,2,128]{3,1,2,0:T(8,128)(2,1)}, bf16[64,8,2,128]{3,1,2,0:T(8,128)(2,1)}, u32[]{:S(2)}, u32[]{:S(2)}) collective-permute-start(bf16[64,8,2,128]{3,1,2,0:T(8,128)(2,1)} %constant_dynamic-update-slice_fusion.113), channel_id=1, source_target_pairs={{256,0},{260,4},{264,8},{268,12},{272,16},{276,20},{280,24},{284,2... | collective-permute-start | bytes 786440 | tf_op jit(solution)/shard_map/ppermute | solution.py:19
  467.9 42.8 %collective-permute-start.92 = (f32[1,8,2]{1,2,0:T(2,128)}, f32[1,8,2]{1,2,0:T(2,128)}, u32[]{:S(2)}, u32[]{:S(2)}) collective-permute-start(f32[1,8,2]{1,2,0:T(2,128)} %bitcast.651), channel_id=1, source_target_pairs={{4,0},{8,4},{12,8},{16,12},{20,16},{24,20},{28,24},{32,28},{36,32}... | collective-permute-start | bytes 200 | tf_op jit(solution)/shard_map/ppermute | solution.py:19
  476.0 38.0 %collective-permute-start.104 = (f32[1,8,2]{1,2,0:T(2,128)}, f32[1,8,2]{1,2,0:T(2,128)}, u32[]{:S(2)}, u32[]{:S(2)}) collective-permute-start(f32[1,8,2]{1,2,0:T(2,128)} %bitcast.642), channel_id=1, source_target_pairs={{4,0},{8,4},{12,8},{16,12},{20,16},{24,20},{28,24},{32,28},{36,32}... | collective-permute-start | bytes 200 | tf_op jit(solution)/shard_map/ppermute | solution.py:19
  506.8 151.0 %collective-permute-start.39 = (f32[1,256,2]{1,2,0:T(2,128)S(1)}, f32[1,256,2]{1,2,0:T(2,128)S(1)}, u32[]{:S(2)}, u32[]{:S(2)}) collective-permute-start(f32[1,256,2]{1,2,0:T(2,128)S(1)} %bitcast.621), channel_id=1, source_target_pairs={{4,0},{8,4},{12,8},{16,12},{20,16},{24,20},{28,24},{32,28},{36,32}... | collective-permute-start | bytes 6152 | tf_op jit(solution)/shard_map/ppermute | solution.py:19
  508.8 318.6 %collective-permute-start.40 = (bf16[1,256,2,128]{1,3,2,0:T(8,128)(2,1)S(1)}, bf16[1,256,2,128]{1,3,2,0:T(8,128)(2,1)}, u32[]{:S(2)}, u32[]{:S(2)}) collective-permute-start(bf16[1,256,2,128]{1,3,2,0:T(8,128)(2,1)S(1)} %bitcast.489), channel_id=1, source_target_pairs={{4,0},{8,4},{12,8},{16,12},{20,16},{24,20},{28,24},{32,28},{36,32}... | collective-permute-start | bytes 393224 | tf_op jit(solution)/shard_map/ppermute | solution.py:19
  519.2 71.6 %collective-permute-start.49 = (f32[1,64,2]{1,2,0:T(2,128)S(1)}, f32[1,64,2]{1,2,0:T(2,128)S(1)}, u32[]{:S(2)}, u32[]{:S(2)}) collective-permute-start(f32[1,64,2]{1,2,0:T(2,128)S(1)} %bitcast.627), channel_id=1, source_target_pairs={{4,0},{8,4},{12,8},{16,12},{20,16},{24,20},{28,24},{32,28},{36,32}... | collective-permute-start | bytes 1544 | tf_op jit(solution)/shard_map/ppermute | solution.py:19
  650.7 76.6 %collective-permute-start.98 = (bf16[1,8,2,128]{3,1,2,0:T(8,128)(2,1)S(1)}, bf16[1,8,2,128]{3,1,2,0:T(8,128)(2,1)S(1)}, u32[]{:S(2)}, u32[]{:S(2)}) collective-permute-start(bf16[1,8,2,128]{3,1,2,0:T(8,128)(2,1)S(1)} %bitcast.601), channel_id=1, source_target_pairs={{4,0},{8,4},{12,8},{16,12},{20,16},{24,20},{28,24},{32,28},{36,32}... | collective-permute-start | bytes 12296 | tf_op jit(solution)/shard_map/ppermute | solution.py:19
  657.8 120.8 %collective-permute-start.72 = (bf16[1,16,2,128]{3,1,2,0:T(8,128)(2,1)S(1)}, bf16[1,16,2,128]{3,1,2,0:T(8,128)(2,1)S(1)}, u32[]{:S(2)}, u32[]{:S(2)}) collective-permute-start(bf16[1,16,2,128]{3,1,2,0:T(8,128)(2,1)S(1)} %bitcast.572), channel_id=1, source_target_pairs={{4,0},{8,4},{12,8},{16,12},{20,16},{24,20},{28,24},{32,28},{36,32}... | collective-permute-start | bytes 24584 | tf_op jit(solution)/shard_map/ppermute | solution.py:19
  716.0 20.3 %collective-permute-start.43 = (f32[2,256,2]{1,2,0:T(2,128)S(1)}, f32[2,256,2]{1,2,0:T(2,128)S(1)}, u32[]{:S(2)}, u32[]{:S(2)}) collective-permute-start(f32[2,256,2]{1,2,0:T(2,128)S(1)} %pad_maximum_fusion.46), channel_id=1, source_target_pairs={{8,0},{12,4},{16,8},{20,12},{24,16},{28,20},{32,24},{36,28},{40,32... | collective-permute-start | bytes 12296 | tf_op jit(solution)/shard_map/ppermute | solution.py:19
  755.9 44.9 %collective-permute-start.52 = (bf16[1,64,2,128]{3,1,2,0:T(8,128)(2,1)S(1)}, bf16[1,64,2,128]{3,1,2,0:T(8,128)(2,1)S(1)}, u32[]{:S(2)}, u32[]{:S(2)}) collective-permute-start(bf16[1,64,2,128]{3,1,2,0:T(8,128)(2,1)S(1)} %bitcast.528), channel_id=1, source_target_pairs={{4,0},{8,4},{12,8},{16,12},{20,16},{24,20},{28,24},{32,28},{36,32}... | collective-permute-start | bytes 98312 | tf_op jit(solution)/shard_map/ppermute | solution.py:19
  761.9 84.9 %collective-permute-start.45 = (f32[2,256,2]{1,2,0:T(2,128)}, f32[2,256,2]{1,2,0:T(2,128)}, u32[]{:S(2)}, u32[]{:S(2)}) collective-permute-start(f32[2,256,2]{1,2,0:T(2,128)} %pad_maximum_fusion.47), channel_id=1, source_target_pairs={{8,0},{12,4},{16,8},{20,12},{24,16},{28,20},{32,24},{36,28},{40,32... | collective-permute-start | bytes 12296 | tf_op jit(solution)/shard_map/ppermute | solution.py:19
  790.6 18.6 %collective-permute-start.74 = (bf16[4,16,2,128]{3,1,2,0:T(8,128)(2,1)S(1)}, bf16[4,16,2,128]{3,1,2,0:T(8,128)(2,1)S(1)}, u32[]{:S(2)}, u32[]{:S(2)}) collective-permute-start(bf16[4,16,2,128]{3,1,2,0:T(8,128)(2,1)S(1)} %pad_maximum_fusion.25), channel_id=1, source_target_pairs={{16,0},{20,4},{24,8},{28,12},{32,16},{36,20},{40,24},{44,28},{48,3... | collective-permute-start | bytes 98312 | tf_op jit(solution)/shard_map/ppermute | solution.py:19
  793.2 21.7 %collective-permute-start.101 = (bf16[8,8,2,128]{3,1,2,0:T(8,128)(2,1)S(1)}, bf16[8,8,2,128]{3,1,2,0:T(8,128)(2,1)S(1)}, u32[]{:S(2)}, u32[]{:S(2)}) collective-permute-start(bf16[8,8,2,128]{3,1,2,0:T(8,128)(2,1)S(1)} %pad_maximum_fusion.27), channel_id=1, source_target_pairs={{32,0},{36,4},{40,8},{44,12},{48,16},{52,20},{56,24},{60,28},{64,3... | collective-permute-start | bytes 98312 | tf_op jit(solution)/shard_map/ppermute | solution.py:19
  826.1 16.7 %collective-permute-start.103 = (bf16[32,8,2,128]{3,1,2,0:T(8,128)(2,1)}, bf16[32,8,2,128]{3,1,2,0:T(8,128)(2,1)}, u32[]{:S(2)}, u32[]{:S(2)}) collective-permute-start(bf16[32,8,2,128]{3,1,2,0:T(8,128)(2,1)} %get-tuple-element.52), channel_id=1, source_target_pairs={{128,0},{132,4},{136,8},{140,12},{144,16},{148,20},{152,24},{156,2... | collective-permute-start | bytes 393224 | tf_op jit(solution)/shard_map/ppermute | solution.py:19
  829.0 16.7 %collective-permute-start.44 = (bf16[2,256,2,128]{1,3,2,0:T(8,128)(2,1)}, bf16[2,256,2,128]{1,3,2,0:T(8,128)(2,1)}, u32[]{:S(2)}, u32[]{:S(2)}) collective-permute-start(bf16[2,256,2,128]{1,3,2,0:T(8,128)(2,1)} %pad_maximum_fusion.5), channel_id=1, source_target_pairs={{8,0},{12,4},{16,8},{20,12},{24,16},{28,20},{32,24},{36,28},{40,32... | collective-permute-start | bytes 786440 | tf_op jit(solution)/shard_map/ppermute | solution.py:19
  844.4 35.2 %collective-permute-start.112 = (bf16[64,8,2,128]{3,1,2,0:T(8,128)(2,1)}, bf16[64,8,2,128]{3,1,2,0:T(8,128)(2,1)}, u32[]{:S(2)}, u32[]{:S(2)}) collective-permute-start(bf16[64,8,2,128]{3,1,2,0:T(8,128)(2,1)} %constant_dynamic-update-slice_fusion.136), channel_id=1, source_target_pairs={{256,0},{260,4},{264,8},{268,12},{272,16},{276,20},{280,24},{284,2... | collective-permute-start | bytes 786440 | tf_op jit(solution)/shard_map/ppermute | solution.py:19
  (322 other events, 3197.5 us)
where the time goes:
time: 897 us; the launch traced here: 890 us
  starting transfers between devices  478 us (53%)
  waiting for transfers between devices  162 us (18%)
  local copies, waits for them, and re-layouts  137 us (15%)
  other arithmetic  43.8 us (5%)
  matrix products  43.2 us (5%)
  blocking collectives  21.3 us (2%)
    ppermute x114, starting transfers between devices, passed_along(): lax.ppermute(value, axis, [(source, source + steps) for source in range(l...  478 us
    ppermute x114, waiting for transfers between devices, passed_along(): lax.ppermute(value, axis, [(source, source + steps) for source in range(l...  162 us
    unnamed x575, local copies, waits for them, and re-layouts  59.3 us
    concatenate x43, local copies, waits for them, and re-layouts, extend(): jnp.concatenate([held, current], axis=0)  25.1 us
    psum x2, blocking collectives, feature_sums(): return lax.psum((first, second), 'head')  21.3 us
    broadcast_in_dim x45, local copies, waits for them, and re-layouts, put_rows(): jnp.where(column == target, compact[:, None], jnp.asarray(filler, compact...  18.8 us
  transfers between devices with their start and end apart: 114, of which 38 were waited for; matrix products, arithmetic and copies ran while one was open for 21% of the time, Pallas kernels for 0%

commit v1 on v0

v1 whole, which is shorter than its diff:
```python
import numpy as np
import jax
import jax.numpy as jnp
from jax import lax
from jax.sharding import Mesh
from jax.sharding import PartitionSpec as P

RATE2 = 4
RATE3 = 16
RATE4 = 32
RATES = (1, RATE2, RATE3, RATE4)

neg_fill = -1e30
epsilon = 1e-05


def pick_rows(source, wanted, stride):
    row_count = source.shape[0] // stride
    shaped = source.reshape((row_count, stride) + source.shape[1:])
    trailing = (1,) * (source.ndim - 2)
    target = wanted.reshape((1, 1, -1) + trailing)
    column = jnp.arange(stride, dtype=jnp.int32).reshape((1, stride, 1) + trailing)
    zeroed = jnp.where(column == target, shaped, jnp.zeros((), source.dtype))
    return jnp.sum(zeroed, axis=1, dtype=source.dtype)


def put_rows(compact, wanted, stride, filler):
    trailing = (1,) * (compact.ndim - 2)
    target = wanted.reshape((1, 1, -1) + trailing)
    column = jnp.arange(stride, dtype=jnp.int32).reshape((1, stride, 1) + trailing)
    spread = jnp.where(column == target, compact[:, None], jnp.asarray(filler, compact.dtype))
    return spread.reshape((compact.shape[0] * stride,) + compact.shape[1:])


def level_plan(tok_dev, seq_count):
    group_rows = tok_dev * seq_count // RATE4
    spans = [max(1, stride * group_rows // tok_dev) for stride in RATES]
    factors = []
    covered = 1
    for span in spans:
        factors.append(span // covered)
        covered = span
    names = tuple("s%d" % (index + 1) for index in range(len(spans)))
    return spans, factors, names


def shards(plan, query_rows, key_rows, value_rows, cotangent, norm_gain, offsets):
    spans, factors, names = plan
    tok_dev, heads_dev, head_size = query_rows.shape
    score_scale = head_size ** (-0.5)
    features = heads_dev * head_size * lax.axis_size("head")
    seq_axes = tuple(reversed(names))
    device = lax.axis_index(seq_axes)

    levels = []
    for index, stride in enumerate(RATES):
        axes = tuple(reversed(names[: index + 1]))
        span = spans[index]
        rows = tok_dev // stride
        wanted = offsets % stride
        place = (device % span) * rows
        key_sel = pick_rows(key_rows, wanted, stride)
        value_sel = pick_rows(value_rows, wanted, stride)
        query_sel = pick_rows(query_rows, wanted, stride)
        packed = jnp.stack([key_sel, value_sel, query_sel], axis=1)
        gathered = lax.all_gather(packed, axes, axis=0, tiled=True)
        levels.append(
            dict(
                stride=stride,
                axes=axes,
                rows=rows,
                wanted=wanted,
                place=place,
                key_sel=key_sel,
                value_sel=value_sel,
                query_sel=query_sel,
                key_all=gathered[:, 0],
                value_all=gathered[:, 1],
                query_all=gathered[:, 2],
            )
        )

    lse_total = jnp.full((tok_dev, heads_dev), neg_fill, jnp.float32)
    for level in levels:
        total_rows = level["key_all"].shape[0]
        raw = (
            jnp.einsum(
                "qhd,khd->hqk", level["query_sel"], level["key_all"],
                preferred_element_type=jnp.float32,
            )
            * score_scale
        )
        query_at = level["place"] + jnp.arange(level["rows"], dtype=jnp.int32)
        key_at = jnp.arange(total_rows, dtype=jnp.int32)
        linked = key_at[None, :] <= query_at[:, None]
        scores = jnp.where(linked[None], raw, neg_fill)
        row_peak = jnp.max(scores, axis=2)
        level_lse = row_peak + jnp.log(jnp.sum(jnp.exp(scores - row_peak[:, :, None]), axis=2))
        level["scores"] = scores
        lse_total = jnp.logaddexp(
            lse_total, put_rows(level_lse.T, level["wanted"], level["stride"], neg_fill)
        )

    attended = jnp.zeros((tok_dev, heads_dev, head_size), jnp.float32)
    for level in levels:
        lse_sel = pick_rows(lse_total, level["wanted"], level["stride"])
        weights = jnp.exp(level["scores"] - lse_sel.T[:, :, None])
        level["lse_sel"] = lse_sel
        level["weights"] = weights
        out_sel = jnp.einsum(
            "hqk,khd->qhd", weights.astype(jnp.bfloat16), level["value_all"],
            preferred_element_type=jnp.float32,
        )
        attended = attended + put_rows(out_sel, level["wanted"], level["stride"], 0.0)

    grad_in = cotangent.astype(jnp.float32) * norm_gain[None]
    sums = lax.psum(
        jnp.stack(
            [
                jnp.sum(attended, axis=(1, 2)),
                jnp.sum(attended * attended, axis=(1, 2)),
                jnp.sum(grad_in, axis=(1, 2)),
                jnp.sum(grad_in * attended, axis=(1, 2)),
            ]
        ),
        "head",
    )
    centre = sums[0] / features
    variance = sums[1] / features - centre * centre
    inverse = lax.rsqrt(variance + epsilon)
    first_mean = sums[2] / features
    second_mean = inverse * (sums[3] / features - centre * first_mean)
    normed = (attended - centre[:, None, None]) * inverse[:, None, None]
    d_attended = (
        inverse[:, None, None]
        * (grad_in - first_mean[:, None, None] - normed * second_mean[:, None, None])
    ).astype(jnp.bfloat16)
    row_delta = jnp.sum(d_attended.astype(jnp.float32) * attended, axis=2)

    query_grad = jnp.zeros((tok_dev, heads_dev, head_size), jnp.float32)
    for level in levels:
        dout_sel = pick_rows(d_attended, level["wanted"], level["stride"])
        delta_sel = pick_rows(row_delta, level["wanted"], level["stride"])
        weight_grad = jnp.einsum(
            "qhd,khd->hqk", dout_sel, level["value_all"], preferred_element_type=jnp.float32
        )
        score_grad = (level["weights"] * (weight_grad - delta_sel.T[:, :, None])).astype(
            jnp.bfloat16
        )
        grad_sel = jnp.einsum(
            "hqk,khd->qhd", score_grad, level["key_all"], preferred_element_type=jnp.float32
        )
        query_grad = query_grad + put_rows(
            grad_sel * score_scale, level["wanted"], level["stride"], 0.0
        )
        level["dout_all"] = lax.all_gather(dout_sel, level["axes"], axis=0, tiled=True)
        stats = jnp.stack([level["lse_sel"], delta_sel], axis=1)
        level["stats_all"] = lax.all_gather(stats, level["axes"], axis=0, tiled=True)

    key_grad = jnp.zeros((tok_dev, heads_dev, head_size), jnp.float32)
    value_grad = jnp.zeros((tok_dev, heads_dev, head_size), jnp.float32)
    for level in levels:
        query_all = level["query_all"]
        dout_all = level["dout_all"]
        lse_all = level["stats_all"][:, 0]
        delta_all = level["stats_all"][:, 1]
        total_rows = query_all.shape[0]
        raw = (
            jnp.einsum(
                "qhd,khd->hqk", query_all, level["key_sel"], preferred_element_type=jnp.float32
            )
            * score_scale
        )
        key_at = level["place"] + jnp.arange(level["rows"], dtype=jnp.int32)
        query_at = jnp.arange(total_rows, dtype=jnp.int32)
        linked = key_at[None, :] <= query_at[:, None]
        scores = jnp.where(linked[None], raw, neg_fill)
        weights = jnp.exp(scores - lse_all.T[:, :, None])
        value_grad_sel = jnp.einsum(
            "hqk,qhd->khd", weights.astype(jnp.bfloat16), dout_all,
            preferred_element_type=jnp.float32,
        )
        weight_grad = jnp.einsum(
            "qhd,khd->hqk", dout_all, level["value_sel"], preferred_element_type=jnp.float32
        )
        score_grad = (weights * (weight_grad - delta_all.T[:, :, None])).astype(jnp.bfloat16)
        key_grad_sel = jnp.einsum(
            "hqk,qhd->khd", score_grad, query_all, preferred_element_type=jnp.float32
        )
        key_grad = key_grad + put_rows(
            key_grad_sel * score_scale, level["wanted"], level["stride"], 0.0
        )
        value_grad = value_grad + put_rows(value_grad_sel, level["wanted"], level["stride"], 0.0)

    return (
        query_grad.astype(jnp.bfloat16),
        key_grad.astype(jnp.bfloat16),
        value_grad.astype(jnp.bfloat16),
    )


def solution(mesh):
    seq_count = mesh.shape["seq"]
    head_count = mesh.shape["head"]

    def run(query_rows, key_rows, value_rows, cotangent, norm_gain, offsets):
        tok_dev = query_rows.shape[0] // seq_count
        plan = level_plan(tok_dev, seq_count)
        spans, factors, names = plan
        grid = np.asarray(mesh.devices).reshape(tuple(reversed(factors)) + (head_count,))
        sub_mesh = Mesh(grid, tuple(reversed(names)) + ("head",))
        seq_spec = tuple(reversed(names))
        rows_spec = P(seq_spec, "head", None)
        placed = (rows_spec, rows_spec, rows_spec, rows_spec, P("head", None), P("head"))

        def body(*args):
            return shards(plan, *args)

        return jax.shard_map(
            body,
            mesh=sub_mesh,
            in_specs=placed,
            out_specs=(rows_spec, rows_spec, rows_spec),
            check_vma=False,
        )(query_rows, key_rows, value_rows, cotangent, norm_gain, offsets)

    return run
```

time: 897 us -> 1190 us (1.33)
  the two profiles are of different devices: /device:TPU:104 before, /device:TPU:6 now
where the time goes in v1:
time: 1190 us; the launch traced here: 1180 us
  blocking collectives  750 us (63%)
  waiting for transfers between devices  321 us (27%)
  local copies, waits for them, and re-layouts  37.1 us (3%)
  matrix products  34 us (3%)
  other arithmetic  20.9 us (2%)
  between operations  14.5 us (1%)
    all_gather x4, blocking collectives, shards(): lax.all_gather(dout_sel, level['axes'], axis=0, tiled=True)  371 us
    all_gather x4, blocking collectives, shards(): lax.all_gather(stats, level['axes'], axis=0, tiled=True)  368 us
    all_gather x4, waiting for transfers between devices, shards(): gathered = lax.all_gather(packed, axes, axis=0, tiled=True)  321 us
  transfers between devices with their start and end apart: 4, of which 4 were waited for; matrix products, arithmetic and copies ran while one was open for 1% of the time, Pallas kernels for 0%

profile of v1, /device:TPU:6, one launch (start us, length us, event | category | flops | bytes accessed | tf_op | source)
XLA Modules:
  0.0 1177.8 jit_solution(1432584091598694713)
XLA Ops:
  7.3 1.0 copy.162
  8.3 1.0 fusion.120
  18.5 25.9 %all-gather.5.cloned.1.call-done = bf16[1024,3,2,128]{3,0,2,1:T(8,128)(2,1)} async-done(((bf16[256,3,2,128]{3,0,2,1:T(8,128)(2,1)}), bf16[1024,3,2,128]{3,0,2,1:T(8,128)(2,1)}) %all-gather.5.cloned.1.call-update) | async-done | bytes 1572880 | tf_op jit(solution)/shard_map/all_gather | solution.py:66
  44.4 1.5 fusion.126
  46.2 65.8 %all-gather.7.cloned.1.call-done = bf16[1024,3,2,128]{3,0,2,1:T(8,128)(2,1)} async-done(((bf16[64,3,2,128]{3,0,2,1:T(8,128)(2,1)}), bf16[1024,3,2,128]{3,0,2,1:T(8,128)(2,1)}) %all-gather.7.cloned.1.call-update) | async-done | bytes 1572880 | tf_op jit(solution)/shard_map/all_gather | solution.py:66
  112.0 1.4 fusion.125
  113.9 123.9 %all-gather.9.cloned.1.call-done = bf16[1024,3,2,128]{3,0,2,1:T(8,128)(2,1)} async-done(((bf16[16,3,2,128]{3,0,2,1:T(8,128)(2,1)}), bf16[1024,3,2,128]{3,0,2,1:T(8,128)(2,1)}) %all-gather.9.cloned.1.call-update) | async-done | bytes 1572880 | tf_op jit(solution)/shard_map/all_gather | solution.py:66
  237.8 1.4 fusion.124
  239.7 105.4 %all-gather.11.cloned.1.call-done = bf16[1024,3,2,128]{3,0,2,1:T(8,128)(2,1)} async-done(((bf16[8,3,2,128]{3,0,2,1:T(8,128)(2,1)}), bf16[1024,3,2,128]{3,0,2,1:T(8,128)(2,1)}) %all-gather.11.cloned.1.call-update) | async-done | bytes 1572880 | tf_op jit(solution)/shard_map/all_gather | solution.py:66
  345.1 1.4 fusion.123
  350.0 1.3 convolution_bitcast_fusion.3
  352.2 1.3 convolution_bitcast_fusion.5
  354.6 1.3 convolution_bitcast_fusion.7
  356.7 1.8 fusion.115
  358.6 11.6 psum.7
  372.6 1.4 select_reduce_fusion
  373.9 1.3 select_reduce_fusion.1
  375.2 6.8 all_gather.41
  383.4 1.3 pad_maximum_fusion.8
  384.7 1.3 copy.123
  386.7 5.2 all_gather.40
  393.8 1.3 pad_maximum_fusion.7
  395.1 1.4 copy.119
  398.0 1.3 pad_maximum_fusion.6
  399.2 1.4 copy.115
  401.5 25.8 %all_gather.43 = bf16[1024,2,128]{2,0,1:T(8,128)(2,1)} all-gather(bf16[64,2,128]{2,0,1:T(8,128)(2,1)S(1)} %select_reduce_fusion.2), channel_id=1, replica_groups=mesh['s4'=2,'s3'=4,'s2'=4,'s1'=4,'head'=4] {'s2','s1'}, dimensions={0}, use_global_device_ids=true | all-gather | bytes 557056 | tf_op jit(solution)/shard_map/all_gather | solution.py:156
  427.4 2.3 fusion.43
  431.4 110.8 %all_gather.45 = bf16[1024,2,128]{2,0,1:T(8,128)(2,1)S(1)} all-gather(bf16[16,2,128]{2,0,1:T(8,128)(2,1)} %select_reduce_fusion.1), channel_id=1, replica_groups=mesh['s4'=2,'s3'=4,'s2'=4,'s1'=4,'head'=4] {'s3','s2','s1'}, dimensions={0}, use_global_device_ids=true | all-gather | bytes 532480 | tf_op jit(solution)/shard_map/all_gather | solution.py:156
  542.3 2.2 fusion.57
  544.5 1.4 broadcast_in_dim.656
  545.9 1.8 copy.108
  547.7 227.2 %all_gather.47 = bf16[1024,2,128]{2,0,1:T(8,128)(2,1)} all-gather(bf16[8,2,128]{2,0,1:T(8,128)(2,1)} %select_reduce_fusion), channel_id=1, replica_groups=mesh['s4'=2,'s3'=4,'s2'=4,'s1'=4,'head'=4] {'s4','s3','s2','s1'}, dimensions={0}, use_global_device_ids=true | all-gather | bytes 528384 | tf_op jit(solution)/shard_map/all_gather | solution.py:156
  775.0 2.2 fusion.63
  777.2 1.4 broadcast_in_dim.658
  778.6 1.8 copy.110
  780.4 2.8 fusion.31
  783.2 1.7 copy.130
  784.9 31.0 %all_gather.42 = f32[1024,2,2]{2,1,0:T(2,128)S(1)} all-gather(f32[64,2,2]{2,1,0:T(2,128)} %copy.115), channel_id=1, replica_groups=mesh['s4'=2,'s3'=4,'s2'=4,'s1'=4,'head'=4] {'s2','s1'}, dimensions={0}, use_global_device_ids=true | all-gather | bytes 17408 | tf_op jit(solution)/shard_map/all_gather | solution.py:158
  817.2 1.4 fusion.6
  819.7 1.5 fusion.45
  822.0 112.5 %all_gather.44 = f32[1024,2,2]{2,1,0:T(2,128)S(1)} all-gather(f32[16,2,2]{2,1,0:T(2,128)S(1)} %copy-done.19), channel_id=1, replica_groups=mesh['s4'=2,'s3'=4,'s2'=4,'s1'=4,'head'=4] {'s3','s2','s1'}, dimensions={0}, use_global_device_ids=true | all-gather | bytes 16640 | tf_op jit(solution)/shard_map/all_gather | solution.py:158
  935.7 1.3 fusion.35
  938.1 1.4 fusion.59
  940.4 219.0 %all_gather.46 = f32[1024,2,2]{2,1,0:T(2,128)S(1)} all-gather(f32[8,2,2]{2,1,0:T(2,128)S(1)} %copy-done.21), channel_id=1, replica_groups=mesh['s4'=2,'s3'=4,'s2'=4,'s1'=4,'head'=4] {'s4','s3','s2','s1'}, dimensions={0}, use_global_device_ids=true | all-gather | bytes 16512 | tf_op jit(solution)/shard_map/all_gather | solution.py:158
  1160.6 1.3 fusion.50
  1163.0 1.4 fusion.61
  1165.3 1.8 subtract_exponential_fusion
  1168.4 2.1 fusion.30
  (223 shorter events, 38.4 us)
Async XLA Ops:
  7.2 5.2 copy-start.3
  7.2 5.2 copy-start.2
  7.2 5.2 copy-start.6
  7.2 3.0 copy-start.51
  7.2 37.2 %all-gather.5.cloned.1.call-start = ((), (), s32[]{:S(2)}) async-start(), calls=%async_computation | async-start | bytes 1966080 | tf_op jit(solution)/shard_map/all_gather | solution.py:66
  9.3 6.4 copy-start.16
  10.2 101.8 %all-gather.7.cloned.1.call-start = ((), (), s32[]{:S(2)}) async-start(), calls=%async_computation.1 | async-start | bytes 1671168 | tf_op jit(solution)/shard_map/all_gather | solution.py:66
  10.3 338.1 %copy-start.38 = (pred[4,2]{0,1:T(4,128)(4,1)}, pred[4,2]{0,1:T(4,128)(4,1)S(1)}, u32[]{:S(2)}) copy-start(pred[4,2]{0,1:T(4,128)(4,1)S(1)} %iota_compare_fusion.10) | copy-start | bytes 28
  12.2 225.6 %all-gather.9.cloned.1.call-start = ((), (), s32[]{:S(2)}) async-start(), calls=%async_computation.2 | async-start | bytes 1597440 | tf_op jit(solution)/shard_map/all_gather | solution.py:66
  12.4 336.7 %copy-start.39 = (pred[16,2]{0,1:T(4,128)(4,1)}, pred[16,2]{0,1:T(4,128)(4,1)S(1)}, u32[]{:S(2)}) copy-start(pred[16,2]{0,1:T(4,128)(4,1)S(1)} %iota_compare_fusion.9) | copy-start | bytes 100
  12.7 2.9 copy-start.24
  13.3 331.8 %all-gather.11.cloned.1.call-start = ((), (), s32[]{:S(2)}) async-start(), calls=%async_computation.3 | async-start | bytes 1585152 | tf_op jit(solution)/shard_map/all_gather | solution.py:66
  13.4 32.5 %copy-start.40 = (pred[32,2]{0,1:T(4,128)(4,1)}, pred[32,2]{0,1:T(4,128)(4,1)S(1)}, u32[]{:S(2)}) copy-start(pred[32,2]{0,1:T(4,128)(4,1)S(1)} %iota_compare_fusion.8) | copy-start | bytes 196
  13.6 1.9 copy-start.35
  14.4 332.4 %copy-start.26 = (pred[256,2]{0,1:T(4,128)(4,1)}, pred[256,2]{0,1:T(4,128)(4,1)S(1)}, u32[]{:S(2)}) copy-start(pred[256,2]{0,1:T(4,128)(4,1)S(1)} %broadcast_in_dim.619) | copy-start | bytes 1540
  15.3 331.4 %copy-start.29 = (pred[256,2]{0,1:T(4,128)(4,1)}, pred[256,2]{0,1:T(4,128)(4,1)S(1)}, u32[]{:S(2)}) copy-start(pred[256,2]{0,1:T(4,128)(4,1)S(1)} %broadcast_in_dim.611) | copy-start | bytes 1540
  15.8 331.0 %copy-start.31 = (pred[256,2]{0,1:T(4,128)(4,1)}, pred[256,2]{0,1:T(4,128)(4,1)S(1)}, u32[]{:S(2)}) copy-start(pred[256,2]{0,1:T(4,128)(4,1)S(1)} %broadcast_in_dim.602) | copy-start | bytes 1540
  239.2 113.1 %copy-start.7 = (f32[2,16,1024]{2,1,0:T(8,128)}, f32[2,16,1024]{2,1,0:T(8,128)S(1)}, u32[]{:S(2)}) copy-start(f32[2,16,1024]{2,1,0:T(8,128)S(1)} %get-tuple-element.59) | copy-start | bytes 393220
  346.4 8.1 copy-start.14
  346.6 3.3 copy-start.33
  348.8 2.6 copy-start.42
  349.9 2.3 copy-start.43
  349.9 4.4 copy-start.23
  349.9 4.4 copy-start.41
  351.3 3.1 copy-start.34
  352.2 4.5 copy-start.27
  354.6 2.2 copy-start.50
  356.7 13.5 %copy-start.46 = (f32[2,128]{1,0:T(2,128)S(1)}, f32[2,128]{1,0:T(2,128)}, u32[]{:S(2)}) copy-start(f32[2,128]{1,0:T(2,128)} %param.10) | copy-start | bytes 3076
  370.4 3.6 copy-start.4
  401.5 25.9 %copy-start.15 = (bf16[64,2,128]{2,0,1:T(8,128)(2,1)}, bf16[64,2,128]{2,0,1:T(8,128)(2,1)S(1)}, u32[]{:S(2)}) copy-start(bf16[64,2,128]{2,0,1:T(8,128)(2,1)S(1)} %select_reduce_fusion.2) | copy-start | bytes 98308
  427.4 114.9 %copy-start.8 = (f32[2,16,1024]{2,1,0:T(8,128)S(1)}, f32[2,16,1024]{2,1,0:T(8,128)}, u32[]{:S(2)}) copy-start(f32[2,16,1024]{2,1,0:T(8,128)} %copy-done.7) | copy-start | bytes 393220
  545.9 234.5 %copy-start.5 = (bf16[256,2,128]{0,2,1:T(8,128)(2,1)S(1)}, bf16[256,2,128]{0,2,1:T(8,128)(2,1)}, u32[]{:S(2)}) copy-start(bf16[256,2,128]{0,2,1:T(8,128)(2,1)} %copy-done.4) | copy-start | bytes 393220
  815.9 1.2 copy-start.18
  815.9 1.2 copy-start.20
  816.8 1.8 copy-start
  817.1 2.5 copy-start.13
  818.8 3.2 copy-start.19
  937.2 3.2 copy-start.21
  1159.4 1.2 copy-start.36
  1159.4 1.2 copy-start.44
  1159.4 2.5 copy-start.1
  1162.0 3.4 copy-start.45
  1165.3 1.9 copy-start.9
  1165.3 1.9 copy-start.10
  1165.3 1.9 copy-start.11
  1165.3 1.9 copy-start.28
  1165.3 1.9 copy-start.30
  1165.3 1.9 copy-start.32
  (8 other events, 6.5 us)
Sparse Core Ops, SparseCore 0:
  10.3 34.0 all-gather.4
  48.3 63.6 all-gather.6
  114.7 123.0 all-gather.8
  242.9 102.1 all-gather.10
